TPU v7x, 32 devices: a whole 2x2x4 slice. The times are simulated.
32 devices in a mesh: ri: 4 (over z), ao: 8 (over y, x, core).
Axes of the slice: x: 2, y: 2, z: 4, core: 2. Of those that a mesh axis runs over, the one named last changes fastest.
Arguments:
- tensor: bfloat16 [512, 256, 256], P('ri', 'ao'), may hold values from -0.5 to 0.5
- live_blocks: int32 [8, 8, 8], P('ri', 'ao'), may hold values 0 or 1
- occ_density: bfloat16 [256, 256], P('ao'), may hold values from -0.375 to 0.375
- virt_density: bfloat16 [256, 256], P('ao'), may hold values from -0.375 to 0.375
- occ_mask: int32 [8, 8], P('ao'), may hold values 0 or 1
- virt_mask: int32 [8, 8], P('ao'), may hold values 0 or 1
- pair_slots: int32 [8, 8], P('ao'), may hold values from 0 to 7, as said below
Outputs:
- polar: float32 [512, 512], P('ri', 'ao')
Inputs may be any that keep to these rules, and one draw needn't show every extreme that they name: pair_slots[b, 0] = b, and the 8 entries of a row are different AO blocks.
All inputs are finite; a program needn't handle non-finite values. No bound on the sum of `live_blocks` or of `occ_mask` or of `virt_mask` on one device may be relied on, other than what follows from the above.
Results may differ from a plain program's by a relative error of at most 0.0041.
Values may be sent and summed in bfloat16 or wider, within the bound.
No kernel may reach another device: no remote copies, remote signals or barrier semaphores. Data moves between devices by JAX's collectives and lax.ppermute only.
A program may use at most 192 MiB of HBM per device.

v0:
```python
import jax
import jax.numpy as jnp
from jax import lax
from jax.experimental.layout import Layout, with_layout_constraint
from jax.sharding import PartitionSpec as P

BS = 32
KS = 8
RB = 64


def screen_density(density, block_mask):
    own_blocks = block_mask.shape[0]
    all_blocks = block_mask.shape[1]
    shaped = density.reshape(own_blocks, BS, all_blocks, BS)
    keeper = block_mask.astype(density.dtype)[:, None, :, None]
    return (shaped * keeper).reshape(density.shape)


def pair_routes(size):
    routes = []
    for dist in range(1, size // 2 + 1):
        if 2 * dist < size:
            route = [(r, (r + dist) % size) for r in range(size)]
        else:
            route = []
            for i in range(size // 2):
                if i % 2 == 0:
                    route.append((i, i + dist))
                else:
                    route.append((i + dist, i))
        recv_from = list(range(size))
        send_to = list(range(size))
        for src, dst in route:
            recv_from[dst] = src
            send_to[src] = dst
        routes.append((route, recv_from, send_to))
    return routes


def mask_slab(slab, live):
    keeper = jnp.repeat(jnp.repeat(live[:, 0, :].astype(slab.dtype), RB, axis=0), BS, axis=1)
    return slab * keeper[:, None, :]


def split_hi_lo(values):
    rounded = lax.reduce_precision(values, exponent_bits=8, mantissa_bits=7)
    return (rounded.astype(jnp.bfloat16), (values - rounded).astype(jnp.bfloat16))


def weight_pair(values):
    hi, lo = split_hi_lo(values)
    both = jnp.stack([hi, lo])
    return both.transpose(2, 3, 0, 1).reshape(values.shape[1] * values.shape[2], -1)


def slab_product(flat, weights):
    out = jnp.dot(flat, weights, preferred_element_type=jnp.float32)
    half = weights.shape[1] // 2
    return out[:, :half] + out[:, half:]


def add_cols(total, part, col_block):
    rows = part.shape[0]
    at = (jnp.int32(0), col_block * rows)
    here = lax.dynamic_slice(total, at, part.shape)
    return lax.dynamic_update_slice(total, here + part, at)


def per_device(tensor, live_blocks, occ_density, virt_density, occ_mask, virt_mask, pair_slots):
    rows = tensor.shape[0]
    assert tensor.shape[1] == BS
    planes = lax.axis_size("ri")
    cycle_size = lax.axis_size("ao")
    plane = lax.axis_index("ri")
    routes = pair_routes(planes)
    own = mask_slab(tensor, live_blocks)
    own_flat = own.reshape(rows, -1)
    lead = rows // 4
    early = [lax.ppermute(own_flat[:lead], "ri", route) for route, _, _ in routes]
    late = [lax.ppermute(own_flat[lead:], "ri", route) for route, _, _ in routes]
    stacked = jnp.stack(
        [screen_density(occ_density, occ_mask), screen_density(virt_density, virt_mask)]
    )
    full = lax.all_gather(stacked, "ao", axis=1, tiled=True)
    ao_total = full.shape[2]
    all_blocks = ao_total // BS
    picked = full.reshape(2, all_blocks, BS, ao_total)[:, pair_slots[0]]
    occ_rows = picked[0].reshape(KS * BS, ao_total)
    virt_rows = picked[1].reshape(KS * BS, ao_total)
    halves = jnp.einsum(
        "prk,dkc->cdrp", own, jnp.stack([occ_rows, virt_rows]), preferred_element_type=jnp.float32
    ).astype(jnp.bfloat16)
    halves = with_layout_constraint(halves, Layout(major_to_minor=(0, 1, 2, 3)))
    halves, early = lax.optimization_barrier((halves, early))
    swapped = lax.all_to_all(halves, "ao", 0, 2, tiled=True)
    occ_t = swapped[:, 0]
    virt_t = swapped[:, 1]
    v_part = jnp.einsum("mn,lnp->plm", virt_rows, occ_t, preferred_element_type=jnp.float32)
    w_part = jnp.einsum("kl,nlq->qnk", occ_rows, virt_t, preferred_element_type=jnp.float32)
    v_weights = weight_pair(v_part)
    w_weights = weight_pair(w_part)
    early_stack = jnp.concatenate(early)
    early_mine = slab_product(early_stack, v_weights)
    with_own = slab_product(jnp.concatenate([own_flat, early_stack]), w_weights)
    diag = with_own[:rows]
    early_theirs = with_own[rows:]
    v_weights, w_weights, diag, early_mine, early_theirs, late = lax.optimization_barrier(
        (v_weights, w_weights, diag, early_mine, early_theirs, late)
    )
    late_stack = jnp.concatenate(late)
    late_mine = slab_product(late_stack, v_weights)
    late_theirs = slab_product(late_stack, w_weights)
    count = len(routes)
    lead = rows // 4
    rest = rows - lead

    def slab_rows(early_part, late_part, index):
        return jnp.concatenate(
            [
                early_part[index * lead : (index + 1) * lead],
                late_part[index * rest : (index + 1) * rest],
            ]
        )

    mine_all = jnp.concatenate([slab_rows(early_mine, late_mine, i) for i in range(count)])
    theirs_all = jnp.concatenate([slab_rows(early_theirs, late_theirs, i) for i in range(count)])
    total = jnp.zeros((rows, planes * rows), jnp.float32)
    total = add_cols(total, diag, plane)
    for index, (route, recv_from, send_to) in enumerate(routes):
        source = jnp.array(recv_from, jnp.int32)[plane]
        target = jnp.array(send_to, jnp.int32)[plane]
        mine = mine_all[index * rows : (index + 1) * rows]
        theirs = theirs_all[index * rows : (index + 1) * rows]
        total = add_cols(total, mine.T, source)
        back = lax.ppermute(theirs, "ri", [(d, s) for s, d in route])
        total = add_cols(total, back, target)
    width = total.shape[1] // cycle_size
    sent = total.reshape(rows, cycle_size, width).transpose(1, 0, 2)
    got = lax.all_to_all(sent, "ao", 0, 0, tiled=True)
    return jnp.sum(got, axis=0)


def solution(mesh):
    placed = (
        P("ri", "ao", None),
        P("ri", "ao", None),
        P("ao", None),
        P("ao", None),
        P("ao", None),
        P("ao", None),
        P("ao", None),
    )
    return jax.shard_map(
        per_device, mesh=mesh, in_specs=placed, out_specs=P("ri", "ao"), check_vma=False
    )
```

profile of v0, /device:TPU:0, one launch (start us, length us, event | category | flops | bytes accessed | tf_op | source)
XLA Modules:
  0.0 131.0 jit_solution(13696888787203270410)
XLA Ops:
  0.0 0.7 convert_element_type.32
  0.7 0.1 copy.40
  1.0 0.1 copy.25
  1.1 1.8 %broadcast_multiply_fusion = bf16[128,32,256]{2,1,0:T(8,128)(2,1)S(1)} fusion(bf16[128,32,256]{2,1,0:T(8,128)(2,1)} %param.11, bf16[128,256]{1,0:T(8,128)(2,1)S(1)} %copy.25), kind=kLoop, calls=%fused_computation.32 | loop fusion | flops 1048576 | bytes 4259840 | tf_op jit(solution)/shard_map/mul | solution.py:43
  3.0 0.3 copy.43
  3.3 3.1 %collective-permute-start = (bf16[32,8192]{1,0:T(8,128)(2,1)S(1)}, bf16[32,8192]{1,0:T(8,128)(2,1)}, u32[]{:S(2)}, u32[]{:S(2)}) collective-permute-start(bf16[32,8192]{1,0:T(8,128)(2,1)S(1)} %bitcast.142), channel_id=1, source_target_pairs={{0,8},{8,16},{16,24},{24,0},{1,9},{9,17},{17,25},{25,1},{2,10},{10... | collective-permute-start | bytes 1572872 | tf_op jit(solution)/shard_map/ppermute | solution.py:80
  6.3 5.3 %collective-permute-start.1 = (bf16[32,8192]{1,0:T(8,128)(2,1)S(1)}, bf16[32,8192]{1,0:T(8,128)(2,1)}, u32[]{:S(2)}, u32[]{:S(2)}) collective-permute-start(bf16[32,8192]{1,0:T(8,128)(2,1)S(1)} %bitcast.143), channel_id=1, source_target_pairs={{0,16},{24,8},{1,17},{25,9},{2,18},{26,10},{3,19},{27,11},{4,20},{... | collective-permute-start | bytes 1572872 | tf_op jit(solution)/shard_map/ppermute | solution.py:80
  11.7 0.1 mul.79
  12.0 9.3 %all_gather.3 = bf16[2,256,256]{2,1,0:T(8,128)(2,1)S(1)} all-gather(bf16[2,32,256]{2,1,0:T(8,128)(2,1)S(1)} %pad_maximum_fusion.2), channel_id=1, replica_groups=mesh['ri'=4,'ao'=8] {'ao'}, dimensions={1}, use_global_device_ids=true | all-gather | bytes 294912 | tf_op jit(solution)/shard_map/all_gather | solution.py:85
  21.3 0.6 gather_fusion
  21.9 0.1 copy.22
  22.0 0.1 copy.23
  22.1 3.2 %fusion.15 = bf16[2,256,128,32]{2,1,3,0:T(8,128)(2,1)S(1)} fusion(bf16[128,32,256]{2,1,0:T(8,128)(2,1)S(1)} %broadcast_multiply_fusion, bf16[1,256,256]{1,2,0:T(8,128)(2,1)S(1)} %copy.23, bf16[1,256,256]{1,2,0:T(8,128)(2,1)S(1)} %copy.22), kind=kOutput, calls=%fused_computation.25 | convolution fusion | flops 1074266112 | bytes 6553600 | tf_op jit(solution)/shard_map/prk,dkc->cdrp/dot_general | solution.py:91
  25.3 4.7 %copy.55 = bf16[2,256,128,32]{2,3,0,1:T(8,128)(2,1)} copy(bf16[2,256,128,32]{2,1,3,0:T(8,128)(2,1)S(1)} %fusion.15) | data formatting | bytes 8388608 | tf_op jit(solution)/shard_map/prk,dkc->cdrp/dot_general | solution.py:91
  30.0 4.6 %all-to-all-start = ((bf16[256,2,32,128]{3,2,1,0:T(8,128)(2,1)}), bf16[256,2,32,128]{3,2,1,0:T(8,128)(2,1)}, u32[]{:S(2)}, u32[]{:S(2)}) async-start(bf16[256,2,32,128]{3,2,1,0:T(8,128)(2,1)} %bitcast.125), calls=%async_computation | async-start | bytes 8388608 | tf_op jit(solution)/shard_map/all_to_all | solution.py:96
  34.7 0.1 slice.119
  34.8 2.2 %copy.47 = bf16[12,8,32,256]{3,1,2,0:T(8,128)(2,1)} copy(bf16[12,8,32,256]{3,2,1,0:T(8,128)(2,1)S(1)} %bitcast.130) | data formatting | bytes 3145728
  37.0 2.2 %collective-permute-start.2 = (bf16[96,8192]{1,0:T(8,128)(2,1)}, bf16[96,8192]{1,0:T(8,128)(2,1)}, u32[]{:S(2)}, u32[]{:S(2)}) collective-permute-start(bf16[96,8192]{1,0:T(8,128)(2,1)} %bitcast.64), channel_id=1, source_target_pairs={{0,8},{8,16},{16,24},{24,0},{1,9},{9,17},{17,25},{25,1},{2,10},{10... | collective-permute-start | bytes 4718600 | tf_op jit(solution)/shard_map/ppermute | solution.py:81
  39.1 3.2 %collective-permute-start.3 = (bf16[96,8192]{1,0:T(8,128)(2,1)}, bf16[96,8192]{1,0:T(8,128)(2,1)}, u32[]{:S(2)}, u32[]{:S(2)}) collective-permute-start(bf16[96,8192]{1,0:T(8,128)(2,1)} %bitcast.64), channel_id=1, source_target_pairs={{0,16},{24,8},{1,17},{25,9},{2,18},{26,10},{3,19},{27,11},{4,20},{... | collective-permute-start | bytes 4718600 | tf_op jit(solution)/shard_map/ppermute | solution.py:81
  42.3 0.6 dynamic_slice.24
  43.6 0.6 dynamic_slice.26
  44.8 0.6 dynamic_slice.28
  46.0 0.6 dynamic_slice.30
  47.2 2.8 %copy.46 = bf16[16,8,32,256]{3,1,2,0:T(8,128)(2,1)} copy(bf16[16,8,32,256]{3,2,1,0:T(8,128)(2,1)S(1)} %bitcast.122) | data formatting | bytes 4194304
  49.9 33.8 %all-to-all-done = bf16[256,2,32,128]{3,2,1,0:T(8,128)(2,1)} async-done(((bf16[256,2,32,128]{3,2,1,0:T(8,128)(2,1)}), bf16[256,2,32,128]{3,2,1,0:T(8,128)(2,1)}, u32[]{:S(2)}, u32[]{:S(2)}) %all-to-all-start) | async-done | bytes 4194336 | tf_op jit(solution)/shard_map/all_to_all | solution.py:96
  83.7 3.3 %copy.28 = bf16[8,32,2,32,128]{4,3,0,2,1:T(8,128)(2,1)S(1)} copy(bf16[8,32,2,32,128]{4,3,2,1,0:T(8,128)(2,1)} %bitcast.16) | data formatting | bytes 8388608 | tf_op jit(solution)/shard_map/all_to_all | solution.py:96
  87.0 0.8 fusion.12
  87.8 0.4 maximum_bitcast_fusion.1
  88.2 2.4 %copy.32 = bf16[32,256,2,128]{1,0,3,2:T(8,128)(2,1)S(1)} copy(bf16[32,256,2,128]{1,3,0,2:T(8,128)(2,1)S(1)} %maximum_bitcast_fusion.1) | data formatting | bytes 8388608 | tf_op jit(solution)/shard_map/transpose | solution.py:54
  90.6 4.3 %copy.45 = bf16[32,8,32,256]{3,1,2,0:T(8,128)(2,1)S(1)} copy(bf16[32,8,32,256]{3,2,1,0:T(8,128)(2,1)S(1)} %bitcast.128) | data formatting | bytes 8388608
  95.0 2.7 %fusion.3 = f32[192,256]{1,0:T(8,128)S(1)} fusion(bf16[8192,256]{0,1:T(8,128)(2,1)S(1)} %bitcast.131, bf16[32,8192]{1,0:T(8,128)(2,1)} %collective-permute-done.1, bf16[32,8192]{1,0:T(8,128)(2,1)} %collective-permute-done, bf16[128,8192]{1,0:T(8,128)(2,1)S(1)} %bitcast.134), kind=kOutput, calls=%fused_computation.11 | convolution fusion | flops 814743552 | bytes 7536640 | tf_op jit(solution)/shard_map/dot_general | solution.py:58
  97.7 1.0 fusion.11
  98.8 0.4 maximum_bitcast_fusion
  99.2 2.4 %copy.30 = bf16[32,256,2,128]{1,0,3,2:T(8,128)(2,1)S(1)} copy(bf16[32,256,2,128]{1,3,0,2:T(8,128)(2,1)S(1)} %maximum_bitcast_fusion) | data formatting | bytes 8388608 | tf_op jit(solution)/shard_map/transpose | solution.py:54
  101.6 4.3 %copy.44 = bf16[32,8,32,256]{3,1,2,0:T(8,128)(2,1)S(1)} copy(bf16[32,8,32,256]{3,2,1,0:T(8,128)(2,1)S(1)} %bitcast.129) | data formatting | bytes 8388608
  105.9 3.4 %fusion.18 = f32[64,256]{1,0:T(8,128)S(1)} fusion(bf16[8192,256]{0,1:T(8,128)(2,1)S(1)} %bitcast.126, bf16[32,8192]{1,0:T(8,128)(2,1)} %collective-permute-done.1, bf16[32,8192]{1,0:T(8,128)(2,1)} %collective-permute-done), kind=kOutput, calls=%fused_computation.28 | convolution fusion | flops 270532608 | bytes 5308416 | tf_op jit(solution)/shard_map/dot_general | solution.py:58
  109.3 1.5 %constant_dynamic-update-slice_fusion.1 = bf16[192,8192]{1,0:T(8,128)(2,1)S(1)} fusion(bf16[96,8192]{1,0:T(8,128)(2,1)} %collective-permute-done.2), kind=kLoop, calls=%fused_computation.55 | loop fusion | bytes 3145728
  110.8 1.5 %constant_dynamic-update-slice_fusion = bf16[192,8192]{1,0:T(8,128)(2,1)S(1)} fusion(bf16[192,8192]{1,0:T(8,128)(2,1)S(1)} %constant_dynamic-update-slice_fusion.1, bf16[96,8192]{1,0:T(8,128)(2,1)} %collective-permute-done.3), kind=kLoop, calls=%fused_computation.54 | loop fusion | bytes 3145728 | tf_op jit(solution)/shard_map/concatenate | solution.py:111
  112.4 1.3 fusion.38
  113.8 0.1 copy.37
  114.0 1.3 collective-permute-start.5
  115.3 0.1 copy.36
  115.5 1.4 %collective-permute-start.4 = (f32[128,128]{0,1:T(8,128)S(1)}, f32[128,128]{0,1:T(8,128)S(1)}, u32[]{:S(2)}, u32[]{:S(2)}) collective-permute-start(f32[128,128]{0,1:T(8,128)S(1)} %pad_maximum_fusion), channel_id=1, source_target_pairs={{8,0},{16,8},{24,16},{0,24},{9,1},{17,9},{25,17},{1,25},{10,2},{18... | collective-permute-start | bytes 196616 | tf_op jit(solution)/shard_map/ppermute | solution.py:136
  116.9 3.7 %fusion.37 = f32[192,256]{1,0:T(8,128)S(1)} fusion(bf16[192,8192]{1,0:T(8,128)(2,1)S(1)} %constant_dynamic-update-slice_fusion, bf16[8192,256]{0,1:T(8,128)(2,1)} %bitcast.127), kind=kOutput, calls=%fused_computation.69 | convolution fusion | flops 805306368 | bytes 7536640 | tf_op jit(solution)/shard_map/dot_general | solution.py:58
  120.7 0.1 copy.33
  120.9 0.1 collective-permute-done.5
  121.1 9.3 %all_to_all.23 = f32[8,128,64]{1,2,0:T(8,128)S(1)} all-to-all(f32[8,128,64]{1,2,0:T(8,128)S(1)} %bitcast.133), channel_id=1, replica_groups=mesh['ri'=4,'ao'=8] {'ao'}, dimensions={0} | all-to-all | bytes 524288 | tf_op jit(solution)/shard_map/all_to_all | solution.py:140
  130.4 0.6 reduce_sum.9
  (63 shorter events, 1.0 us)
Async XLA Ops:
  1.1 10.5 %copy-start.5 = (s32[1,8]{1,0:T(1,128)S(1)}, s32[1,8]{1,0:T(1,128)}, u32[]{:S(2)}) copy-start(s32[1,8]{1,0:T(1,128)} %param.15) | copy-start | bytes 100
  1.1 10.7 %copy-start.6 = (s32[1,8]{1,0:T(1,128)S(1)}, s32[1,8]{1,0:T(1,128)}, u32[]{:S(2)}) copy-start(s32[1,8]{1,0:T(1,128)} %param.16) | copy-start | bytes 100
  1.1 10.9 %copy-start.3 = (bf16[32,256]{1,0:T(8,128)(2,1)S(1)}, bf16[32,256]{1,0:T(8,128)(2,1)}, u32[]{:S(2)}) copy-start(bf16[32,256]{1,0:T(8,128)(2,1)} %param.14) | copy-start | bytes 49156
  1.1 10.8 %copy-start.4 = (bf16[32,256]{1,0:T(8,128)(2,1)S(1)}, bf16[32,256]{1,0:T(8,128)(2,1)}, u32[]{:S(2)}) copy-start(bf16[32,256]{1,0:T(8,128)(2,1)} %param.13) | copy-start | bytes 49156
  1.1 20.2 %copy-start.7 = (s32[1,8]{1,0:T(1,128)S(1)}, s32[1,8]{1,0:T(1,128)}, u32[]{:S(2)}) copy-start(s32[1,8]{1,0:T(1,128)} %param.17) | copy-start | bytes 100
  3.3 26.8 %collective-permute-start = (bf16[32,8192]{1,0:T(8,128)(2,1)S(1)}, bf16[32,8192]{1,0:T(8,128)(2,1)}, u32[]{:S(2)}, u32[]{:S(2)}) collective-permute-start(bf16[32,8192]{1,0:T(8,128)(2,1)S(1)} %bitcast.142), channel_id=1, source_target_pairs={{0,8},{8,16},{16,24},{24,0},{1,9},{9,17},{17,25},{25,1},{2,10},{10... | collective-permute-start | bytes 1572872 | tf_op jit(solution)/shard_map/ppermute | solution.py:80
  6.3 23.7 %collective-permute-start.1 = (bf16[32,8192]{1,0:T(8,128)(2,1)S(1)}, bf16[32,8192]{1,0:T(8,128)(2,1)}, u32[]{:S(2)}, u32[]{:S(2)}) collective-permute-start(bf16[32,8192]{1,0:T(8,128)(2,1)S(1)} %bitcast.143), channel_id=1, source_target_pairs={{0,16},{24,8},{1,17},{25,9},{2,18},{26,10},{3,19},{27,11},{4,20},{... | collective-permute-start | bytes 1572872 | tf_op jit(solution)/shard_map/ppermute | solution.py:80
  30.0 53.7 %all-to-all-start = ((bf16[256,2,32,128]{3,2,1,0:T(8,128)(2,1)}), bf16[256,2,32,128]{3,2,1,0:T(8,128)(2,1)}, u32[]{:S(2)}, u32[]{:S(2)}) async-start(bf16[256,2,32,128]{3,2,1,0:T(8,128)(2,1)} %bitcast.125), calls=%async_computation | async-start | bytes 8388608 | tf_op jit(solution)/shard_map/all_to_all | solution.py:96
  34.6 7.7 %copy-start.11 = (s32[4]{0:T(128)S(1)}, s32[4]{0:T(128)}, u32[]{:S(2)}) copy-start(s32[4]{0:T(128)} %constant.32.clone) | copy-start | bytes 52
  34.6 8.9 %copy-start.10 = (s32[4]{0:T(128)S(1)}, s32[4]{0:T(128)}, u32[]{:S(2)}) copy-start(s32[4]{0:T(128)} %constant.33.clone) | copy-start | bytes 52
  34.6 10.2 %copy-start.9 = (s32[4]{0:T(128)S(1)}, s32[4]{0:T(128)}, u32[]{:S(2)}) copy-start(s32[4]{0:T(128)} %constant.34.clone) | copy-start | bytes 52
  34.7 11.3 %copy-start.8 = (s32[4]{0:T(128)S(1)}, s32[4]{0:T(128)}, u32[]{:S(2)}) copy-start(s32[4]{0:T(128)} %constant.35.clone) | copy-start | bytes 52
  37.0 72.3 %collective-permute-start.2 = (bf16[96,8192]{1,0:T(8,128)(2,1)}, bf16[96,8192]{1,0:T(8,128)(2,1)}, u32[]{:S(2)}, u32[]{:S(2)}) collective-permute-start(bf16[96,8192]{1,0:T(8,128)(2,1)} %bitcast.64), channel_id=1, source_target_pairs={{0,8},{8,16},{16,24},{24,0},{1,9},{9,17},{17,25},{25,1},{2,10},{10... | collective-permute-start | bytes 4718600 | tf_op jit(solution)/shard_map/ppermute | solution.py:81
  39.1 70.2 %collective-permute-start.3 = (bf16[96,8192]{1,0:T(8,128)(2,1)}, bf16[96,8192]{1,0:T(8,128)(2,1)}, u32[]{:S(2)}, u32[]{:S(2)}) collective-permute-start(bf16[96,8192]{1,0:T(8,128)(2,1)} %bitcast.64), channel_id=1, source_target_pairs={{0,16},{24,8},{1,17},{25,9},{2,18},{26,10},{3,19},{27,11},{4,20},{... | collective-permute-start | bytes 4718600 | tf_op jit(solution)/shard_map/ppermute | solution.py:81
  90.6 4.3 %copy-start.1 = (bf16[16,8,32,256]{3,1,2,0:T(8,128)(2,1)S(1)}, bf16[16,8,32,256]{3,1,2,0:T(8,128)(2,1)}, u32[]{:S(2)}) copy-start(bf16[16,8,32,256]{3,1,2,0:T(8,128)(2,1)} %copy.46) | copy-start | bytes 6291460
  97.7 1.0 copy-start.2
  105.9 4.9 %copy-start = (bf16[32,8,32,256]{3,1,2,0:T(8,128)(2,1)}, bf16[32,8,32,256]{3,1,2,0:T(8,128)(2,1)S(1)}, u32[]{:S(2)}) copy-start(bf16[32,8,32,256]{3,1,2,0:T(8,128)(2,1)S(1)} %copy.44) | copy-start | bytes 12582916
  112.4 1.4 %slice-start.1 = ((f32[192,128]{1,0:T(8,128)}), f32[64,128]{1,0:T(8,128)S(1)}, s32[]{:S(2)}) async-start(f32[192,128]{1,0:T(8,128)} %copy-done.2), calls=%async_computation.3 | async-start | bytes 65536 | tf_op jit(solution)/shard_map/slice | solution.py:107
  114.0 7.1 %collective-permute-start.5 = (f32[128,128]{0,1:T(8,128)S(1)}, f32[128,128]{0,1:T(8,128)S(1)}, u32[]{:S(2)}, u32[]{:S(2)}) collective-permute-start(f32[128,128]{0,1:T(8,128)S(1)} %pad_maximum_fusion.1), channel_id=1, source_target_pairs={{16,0},{8,24},{17,1},{9,25},{18,2},{10,26},{19,3},{11,27},{20,4},{... | collective-permute-start | bytes 196616 | tf_op jit(solution)/shard_map/ppermute | solution.py:136
  115.5 5.2 %slice-start = ((f32[192,128]{1,0:T(8,128)}), f32[128,128]{1,0:T(8,128)S(1)}, s32[]{:S(2)}) async-start(f32[192,128]{1,0:T(8,128)} %copy-done.2), calls=%async_computation.2 | async-start | bytes 131072 | tf_op jit(solution)/shard_map/slice | solution.py:106
  115.5 5.4 %collective-permute-start.4 = (f32[128,128]{0,1:T(8,128)S(1)}, f32[128,128]{0,1:T(8,128)S(1)}, u32[]{:S(2)}, u32[]{:S(2)}) collective-permute-start(f32[128,128]{0,1:T(8,128)S(1)} %pad_maximum_fusion), channel_id=1, source_target_pairs={{8,0},{16,8},{24,16},{0,24},{9,1},{17,9},{25,17},{1,25},{10,2},{18... | collective-permute-start | bytes 196616 | tf_op jit(solution)/shard_map/ppermute | solution.py:136
where the time goes:
time: 132 us; the launch traced here: 131 us
  local copies, waits for them, and re-layouts  34.2 us (26%)
  waiting for transfers between devices  33.9 us (26%)
  starting transfers between devices  21 us (16%)
  blocking collectives  18.7 us (14%)
  matrix products  16.1 us (12%)
  other arithmetic  4.17 us (3%)
  between operations  2.98 us (2%)
    all_to_all x1, waiting for transfers between devices, per_device(): swapped = lax.all_to_all(halves, 'ao', 0, 2, tiled=True)  33.8 us
    unnamed x30, local copies, waits for them, and re-layouts  15.4 us
    dot_general x4, matrix products, slab_product(): out = jnp.dot(flat, weights, preferred_element_type=jnp.float32)  11.1 us
    all_to_all x1, blocking collectives, per_device(): got = lax.all_to_all(sent, 'ao', 0, 0, tiled=True)  9.35 us
    all_gather x1, blocking collectives, per_device(): full = lax.all_gather(stacked, 'ao', axis=1, tiled=True)  9.32 us
    ppermute x2, starting transfers between devices, per_device(): lax.ppermute(own_flat[:lead], 'ri', route)  8.36 us
    ppermute x2, starting transfers between devices, per_device(): lax.ppermute(own_flat[lead:], 'ri', route)  5.36 us
    transpose x2, local copies, waits for them, and re-layouts, weight_pair(): both.transpose(2, 3, 0, 1).reshape(values.shape[1] * values.shape[2], -1)  4.86 us
  transfers between devices with their start and end apart: 7, of which 2 were waited for; matrix products, arithmetic and copies ran while one was open for 35% of the time, Pallas kernels for 0%

commit v1 on v0

--- a/solution.py
+++ b/solution.py
@@ -82,7 +82,15 @@
     stacked = jnp.stack(
         [screen_density(occ_density, occ_mask), screen_density(virt_density, virt_mask)]
     )
-    full = lax.all_gather(stacked, "ao", axis=1, tiled=True)
+    ways, here_2, hop = (lax.axis_size("ao"), lax.axis_index("ao"), stacked.shape[1])
+    line, have = (stacked, 1)
+    while have < ways:
+        line = jnp.concatenate(
+            [line, lax.ppermute(line, "ao", [(d_2, (d_2 - have) % ways) for d_2 in range(ways)])],
+            axis=1,
+        )
+        have = 2 * have
+    full = jnp.roll(line, here_2 * hop, axis=1)
     ao_total = full.shape[2]
     all_blocks = ao_total // BS
     picked = full.reshape(2, all_blocks, BS, ao_total)[:, pair_slots[0]]

time: 132 us -> 141 us (1.068)
  waiting for transfers between devices: 33.9 us -> 43.4 us
  blocking collectives: 18.7 us -> 9.35 us
  local copies, waits for them, and re-layouts: 34.2 us -> 39.4 us
  starting transfers between devices: 21 us -> 22.9 us
    all_gather x1 -> x0, blocking collectives: 9.32 us -> none  [per_device(): full = lax.all_gather(stacked, 'ao', axis=1, tiled=True)]
    ppermute x0 -> x3, waiting for transfers between devices: none -> 9.27 us  [per_device(): lax.ppermute(line, 'ao', [(d_2, (d_2 - have) % ways) for d_2 in range(way...]
    unnamed x30 -> x37, local copies, waits for them, and re-layouts: 15.4 us -> 19 us
    ppermute x0 -> x3, starting transfers between devices: none -> 2.55 us  [per_device(): lax.ppermute(line, 'ao', [(d_2, (d_2 - have) % ways) for d_2 in range(way...]
  transfers between devices with their start and end apart: 7 -> 10, of which waited for: 2 -> 4; matrix products, arithmetic and copies ran while one was open for 35% -> 38% of each run, Pallas kernels for 0% -> 0%
where the time goes in v1:
time: 141 us
  waiting for transfers between devices  43.4 us (31%)
  local copies, waits for them, and re-layouts  39.4 us (28%)
  starting transfers between devices  22.9 us (16%)
  matrix products  17 us (12%)
  blocking collectives  9.35 us (7%)
  other arithmetic  5.43 us (4%)
  between operations  3.1 us (2%)
    all_to_all x1, waiting for transfers between devices, per_device(): swapped = lax.all_to_all(halves, 'ao', 0, 2, tiled=True)  34.1 us
    unnamed x37, local copies, waits for them, and re-layouts  19 us
    dot_general x4, matrix products, slab_product(): out = jnp.dot(flat, weights, preferred_element_type=jnp.float32)  12 us
    all_to_all x1, blocking collectives, per_device(): got = lax.all_to_all(sent, 'ao', 0, 0, tiled=True)  9.35 us
    ppermute x3, waiting for transfers between devices, per_device(): lax.ppermute(line, 'ao', [(d_2, (d_2 - have) % ways) for d_2 in range(way...  9.27 us
    ppermute x2, starting transfers between devices, per_device(): lax.ppermute(own_flat[:lead], 'ri', route)  8.35 us
    transpose x2, local copies, waits for them, and re-layouts, weight_pair(): both.transpose(2, 3, 0, 1).reshape(values.shape[1] * values.shape[2], -1)  4.86 us
    ppermute x2, starting transfers between devices, per_device(): lax.ppermute(own_flat[lead:], 'ri', route)  4.85 us
  transfers between devices with their start and end apart: 10, of which 4 were waited for; matrix products, arithmetic and copies ran while one was open for 38% of the time, Pallas kernels for 0%

profile of v1, /device:TPU:0, one launch (start us, length us, event | category | flops | bytes accessed | tf_op | source)
XLA Modules:
  0.0 140.6 jit_solution(1553448486775162626)
XLA Ops:
  0.0 0.7 convert_element_type.32
  1.1 1.8 %broadcast_multiply_fusion = bf16[128,32,256]{2,1,0:T(8,128)(2,1)S(1)} fusion(bf16[128,32,256]{2,1,0:T(8,128)(2,1)} %param.11, bf16[128,256]{1,0:T(8,128)(2,1)S(1)} %copy.25), kind=kLoop, calls=%fused_computation.32 | loop fusion | flops 1048576 | bytes 4259840 | tf_op jit(solution)/shard_map/mul | solution.py:43
  3.3 3.1 %collective-permute-start.3 = (bf16[32,8192]{1,0:T(8,128)(2,1)S(1)}, bf16[32,8192]{1,0:T(8,128)(2,1)}, u32[]{:S(2)}, u32[]{:S(2)}) collective-permute-start(bf16[32,8192]{1,0:T(8,128)(2,1)S(1)} %bitcast.142), channel_id=1, source_target_pairs={{0,8},{8,16},{16,24},{24,0},{1,9},{9,17},{17,25},{25,1},{2,10},{10... | collective-permute-start | bytes 1572872 | tf_op jit(solution)/shard_map/ppermute | solution.py:80
  6.3 5.3 %collective-permute-start.4 = (bf16[32,8192]{1,0:T(8,128)(2,1)S(1)}, bf16[32,8192]{1,0:T(8,128)(2,1)}, u32[]{:S(2)}, u32[]{:S(2)}) collective-permute-start(bf16[32,8192]{1,0:T(8,128)(2,1)S(1)} %bitcast.143), channel_id=1, source_target_pairs={{0,16},{24,8},{1,17},{25,9},{2,18},{26,10},{3,19},{27,11},{4,20},{... | collective-permute-start | bytes 1572872 | tf_op jit(solution)/shard_map/ppermute | solution.py:80
  12.0 0.6 pad_maximum_fusion.4
  12.6 1.3 collective-permute-start
  13.9 1.6 %collective-permute-done = bf16[2,32,256]{2,1,0:T(8,128)(2,1)S(1)} collective-permute-done((bf16[2,32,256]{2,1,0:T(8,128)(2,1)S(1)}, bf16[2,32,256]{2,1,0:T(8,128)(2,1)S(1)}, u32[]{:S(2)}, u32[]{:S(2)}) %collective-permute-start) | collective-permute-done | bytes 32800 | tf_op jit(solution)/shard_map/ppermute | solution.py:89
  15.5 1.1 collective-permute-start.1
  16.6 3.6 %collective-permute-done.1 = bf16[2,64,256]{2,1,0:T(8,128)(2,1)S(1)} collective-permute-done((bf16[2,64,256]{2,1,0:T(8,128)(2,1)S(1)}, bf16[2,64,256]{2,1,0:T(8,128)(2,1)S(1)}, u32[]{:S(2)}, u32[]{:S(2)}) %collective-permute-start.1) | collective-permute-done | bytes 65568 | tf_op jit(solution)/shard_map/ppermute | solution.py:89
  20.4 0.6 constant_dynamic-update-slice_fusion.6
  21.0 0.7 constant_dynamic-update-slice_fusion.5
  21.6 4.1 %collective-permute-done.2 = bf16[2,128,256]{2,1,0:T(8,128)(2,1)S(1)} collective-permute-done((bf16[2,128,256]{2,1,0:T(8,128)(2,1)S(1)}, bf16[2,128,256]{2,1,0:T(8,128)(2,1)S(1)}, u32[]{:S(2)}, u32[]{:S(2)}) %collective-permute-start.2) | collective-permute-done | bytes 131104 | tf_op jit(solution)/shard_map/ppermute | solution.py:89
  25.7 0.7 constant_dynamic-update-slice_fusion.4
  26.4 0.6 constant_dynamic-update-slice_fusion.3
  27.0 0.6 constant_dynamic-update-slice_fusion.2
  27.6 0.6 constant_dynamic-update-slice_fusion.1
  28.2 0.7 constant_dynamic-update-slice_fusion
  28.9 1.0 constant_dynamic-slice_fusion
  29.9 0.6 gather_fusion
  30.7 3.2 %fusion.15 = bf16[2,256,128,32]{2,1,3,0:T(8,128)(2,1)S(1)} fusion(bf16[128,32,256]{2,1,0:T(8,128)(2,1)S(1)} %broadcast_multiply_fusion, bf16[1,256,256]{1,2,0:T(8,128)(2,1)S(1)} %copy.23, bf16[1,256,256]{1,2,0:T(8,128)(2,1)S(1)} %copy.22), kind=kOutput, calls=%fused_computation.25 | convolution fusion | flops 1074266112 | bytes 6553600 | tf_op jit(solution)/shard_map/prk,dkc->cdrp/dot_general | solution.py:99
  33.8 4.7 %copy.55 = bf16[2,256,128,32]{2,3,0,1:T(8,128)(2,1)} copy(bf16[2,256,128,32]{2,1,3,0:T(8,128)(2,1)S(1)} %fusion.15) | data formatting | bytes 8388608 | tf_op jit(solution)/shard_map/prk,dkc->cdrp/dot_general | solution.py:99
  38.6 4.6 %all-to-all-start = ((bf16[256,2,32,128]{3,2,1,0:T(8,128)(2,1)}), bf16[256,2,32,128]{3,2,1,0:T(8,128)(2,1)}, u32[]{:S(2)}, u32[]{:S(2)}) async-start(bf16[256,2,32,128]{3,2,1,0:T(8,128)(2,1)} %bitcast.125), calls=%async_computation | async-start | bytes 8388608 | tf_op jit(solution)/shard_map/all_to_all | solution.py:104
  43.3 2.2 %copy.47 = bf16[12,8,32,256]{3,1,2,0:T(8,128)(2,1)} copy(bf16[12,8,32,256]{3,2,1,0:T(8,128)(2,1)S(1)} %bitcast.130) | data formatting | bytes 3145728
  45.5 4.8 %collective-permute-start.6 = (bf16[96,8192]{1,0:T(8,128)(2,1)}, bf16[96,8192]{1,0:T(8,128)(2,1)}, u32[]{:S(2)}, u32[]{:S(2)}) collective-permute-start(bf16[96,8192]{1,0:T(8,128)(2,1)} %bitcast.64), channel_id=1, source_target_pairs={{0,16},{24,8},{1,17},{25,9},{2,18},{26,10},{3,19},{27,11},{4,20},{... | collective-permute-start | bytes 4718600 | tf_op jit(solution)/shard_map/ppermute | solution.py:81
  50.3 0.6 dynamic_slice.29
  51.6 0.6 dynamic_slice.31
  52.8 0.6 dynamic_slice.33
  54.1 0.6 dynamic_slice.35
  55.3 2.8 %copy.46 = bf16[16,8,32,256]{3,1,2,0:T(8,128)(2,1)} copy(bf16[16,8,32,256]{3,2,1,0:T(8,128)(2,1)S(1)} %bitcast.122) | data formatting | bytes 4194304
  58.1 34.1 %all-to-all-done = bf16[256,2,32,128]{3,2,1,0:T(8,128)(2,1)} async-done(((bf16[256,2,32,128]{3,2,1,0:T(8,128)(2,1)}), bf16[256,2,32,128]{3,2,1,0:T(8,128)(2,1)}, u32[]{:S(2)}, u32[]{:S(2)}) %all-to-all-start) | async-done | bytes 4194336 | tf_op jit(solution)/shard_map/all_to_all | solution.py:104
  92.2 3.3 %copy.28 = bf16[8,32,2,32,128]{4,3,0,2,1:T(8,128)(2,1)S(1)} copy(bf16[8,32,2,32,128]{4,3,2,1,0:T(8,128)(2,1)} %bitcast.16) | data formatting | bytes 8388608 | tf_op jit(solution)/shard_map/all_to_all | solution.py:104
  95.5 0.8 fusion.12
  96.7 2.4 %copy.32 = bf16[32,256,2,128]{1,0,3,2:T(8,128)(2,1)S(1)} copy(bf16[32,256,2,128]{1,3,0,2:T(8,128)(2,1)S(1)} %maximum_bitcast_fusion.1) | data formatting | bytes 8388608 | tf_op jit(solution)/shard_map/transpose | solution.py:54
  99.1 4.3 %copy.45 = bf16[32,8,32,256]{3,1,2,0:T(8,128)(2,1)S(1)} copy(bf16[32,8,32,256]{3,2,1,0:T(8,128)(2,1)S(1)} %bitcast.128) | data formatting | bytes 8388608
  103.5 2.7 %fusion.3 = f32[192,256]{1,0:T(8,128)S(1)} fusion(bf16[8192,256]{0,1:T(8,128)(2,1)S(1)} %bitcast.131, bf16[32,8192]{1,0:T(8,128)(2,1)} %collective-permute-done.4, bf16[32,8192]{1,0:T(8,128)(2,1)} %collective-permute-done.3, bf16[128,8192]{1,0:T(8,128)(2,1)S(1)} %bitcast.134), kind=kOutput, calls=%fused_computation.11 | convolution fusion | flops 814743552 | bytes 7536640 | tf_op jit(solution)/shard_map/dot_general | solution.py:58
  106.2 1.0 fusion.11
  107.3 0.4 maximum_bitcast_fusion
  107.7 2.4 %copy.30 = bf16[32,256,2,128]{1,0,3,2:T(8,128)(2,1)S(1)} copy(bf16[32,256,2,128]{1,3,0,2:T(8,128)(2,1)S(1)} %maximum_bitcast_fusion) | data formatting | bytes 8388608 | tf_op jit(solution)/shard_map/transpose | solution.py:54
  110.1 4.3 %copy.44 = bf16[32,8,32,256]{3,1,2,0:T(8,128)(2,1)S(1)} copy(bf16[32,8,32,256]{3,2,1,0:T(8,128)(2,1)S(1)} %bitcast.129) | data formatting | bytes 8388608
  114.4 3.4 %fusion.18 = f32[64,256]{1,0:T(8,128)S(1)} fusion(bf16[8192,256]{0,1:T(8,128)(2,1)S(1)} %bitcast.126, bf16[32,8192]{1,0:T(8,128)(2,1)} %collective-permute-done.4, bf16[32,8192]{1,0:T(8,128)(2,1)} %collective-permute-done.3), kind=kOutput, calls=%fused_computation.28 | convolution fusion | flops 270532608 | bytes 5308416 | tf_op jit(solution)/shard_map/dot_general | solution.py:58
  117.8 1.5 %constant_dynamic-update-slice_fusion.9 = bf16[192,8192]{1,0:T(8,128)(2,1)S(1)} fusion(bf16[96,8192]{1,0:T(8,128)(2,1)} %collective-permute-done.5), kind=kLoop, calls=%fused_computation.62 | loop fusion | bytes 3145728
  119.3 1.5 %constant_dynamic-update-slice_fusion.8 = bf16[192,8192]{1,0:T(8,128)(2,1)S(1)} fusion(bf16[192,8192]{1,0:T(8,128)(2,1)S(1)} %constant_dynamic-update-slice_fusion.9, bf16[96,8192]{1,0:T(8,128)(2,1)} %collective-permute-done.6), kind=kLoop, calls=%fused_computation.61 | loop fusion | bytes 3145728 | tf_op jit(solution)/shard_map/concatenate | solution.py:119
  120.9 1.3 fusion.38
  122.8 1.3 collective-permute-start.8
  124.3 1.3 collective-permute-start.7
  125.6 4.7 %fusion.37 = f32[192,256]{1,0:T(8,128)S(1)} fusion(bf16[192,8192]{1,0:T(8,128)(2,1)} %copy-done.2, bf16[8192,256]{0,1:T(8,128)(2,1)} %bitcast.127), kind=kOutput, calls=%fused_computation.80 | convolution fusion | flops 805306368 | bytes 7536640 | tf_op jit(solution)/shard_map/dot_general | solution.py:58
  130.6 9.3 %all_to_all.23 = f32[8,128,64]{1,2,0:T(8,128)S(1)} all-to-all(f32[8,128,64]{1,2,0:T(8,128)S(1)} %bitcast.133), channel_id=1, replica_groups=mesh['ri'=4,'ao'=8] {'ao'}, dimensions={0} | all-to-all | bytes 524288 | tf_op jit(solution)/shard_map/all_to_all | solution.py:148
  140.0 0.6 reduce_sum.9
  (80 shorter events, 3.1 us)
Async XLA Ops:
  1.1 10.5 %copy-start.6 = (s32[1,8]{1,0:T(1,128)S(1)}, s32[1,8]{1,0:T(1,128)}, u32[]{:S(2)}) copy-start(s32[1,8]{1,0:T(1,128)} %param.15) | copy-start | bytes 100
  1.1 10.7 %copy-start.7 = (s32[1,8]{1,0:T(1,128)S(1)}, s32[1,8]{1,0:T(1,128)}, u32[]{:S(2)}) copy-start(s32[1,8]{1,0:T(1,128)} %param.16) | copy-start | bytes 100
  1.1 10.9 %copy-start.4 = (bf16[32,256]{1,0:T(8,128)(2,1)S(1)}, bf16[32,256]{1,0:T(8,128)(2,1)}, u32[]{:S(2)}) copy-start(bf16[32,256]{1,0:T(8,128)(2,1)} %param.14) | copy-start | bytes 49156
  1.1 10.8 %copy-start.5 = (bf16[32,256]{1,0:T(8,128)(2,1)S(1)}, bf16[32,256]{1,0:T(8,128)(2,1)}, u32[]{:S(2)}) copy-start(bf16[32,256]{1,0:T(8,128)(2,1)} %param.13) | copy-start | bytes 49156
  1.1 12.8 %copy-start.8 = (s32[1,8]{1,0:T(1,128)S(1)}, s32[1,8]{1,0:T(1,128)}, u32[]{:S(2)}) copy-start(s32[1,8]{1,0:T(1,128)} %param.17) | copy-start | bytes 100
  3.3 35.3 %collective-permute-start.3 = (bf16[32,8192]{1,0:T(8,128)(2,1)S(1)}, bf16[32,8192]{1,0:T(8,128)(2,1)}, u32[]{:S(2)}, u32[]{:S(2)}) collective-permute-start(bf16[32,8192]{1,0:T(8,128)(2,1)S(1)} %bitcast.142), channel_id=1, source_target_pairs={{0,8},{8,16},{16,24},{24,0},{1,9},{9,17},{17,25},{25,1},{2,10},{10... | collective-permute-start | bytes 1572872 | tf_op jit(solution)/shard_map/ppermute | solution.py:80
  6.3 32.2 %collective-permute-start.4 = (bf16[32,8192]{1,0:T(8,128)(2,1)S(1)}, bf16[32,8192]{1,0:T(8,128)(2,1)}, u32[]{:S(2)}, u32[]{:S(2)}) collective-permute-start(bf16[32,8192]{1,0:T(8,128)(2,1)S(1)} %bitcast.143), channel_id=1, source_target_pairs={{0,16},{24,8},{1,17},{25,9},{2,18},{26,10},{3,19},{27,11},{4,20},{... | collective-permute-start | bytes 1572872 | tf_op jit(solution)/shard_map/ppermute | solution.py:80
  12.6 2.9 %collective-permute-start = (bf16[2,32,256]{2,1,0:T(8,128)(2,1)S(1)}, bf16[2,32,256]{2,1,0:T(8,128)(2,1)S(1)}, u32[]{:S(2)}, u32[]{:S(2)}) collective-permute-start(bf16[2,32,256]{2,1,0:T(8,128)(2,1)S(1)} %get-tuple-element.39), channel_id=1, source_target_pairs={{0,7},{1,0},{2,1},{3,2},{4,3},{5,4},{6,5},{7,6},{8,15},{9,8},{10,9... | collective-permute-start | bytes 98312 | tf_op jit(solution)/shard_map/ppermute | solution.py:89
  15.5 4.7 %collective-permute-start.1 = (bf16[2,64,256]{2,1,0:T(8,128)(2,1)S(1)}, bf16[2,64,256]{2,1,0:T(8,128)(2,1)S(1)}, u32[]{:S(2)}, u32[]{:S(2)}) collective-permute-start(bf16[2,64,256]{2,1,0:T(8,128)(2,1)S(1)} %pad_maximum_fusion.1), channel_id=1, source_target_pairs={{0,6},{1,7},{2,0},{3,1},{4,2},{5,3},{6,4},{7,5},{8,14},{9,15},{10,... | collective-permute-start | bytes 196616 | tf_op jit(solution)/shard_map/ppermute | solution.py:89
  20.3 5.5 %collective-permute-start.2 = (bf16[2,128,256]{2,1,0:T(8,128)(2,1)S(1)}, bf16[2,128,256]{2,1,0:T(8,128)(2,1)S(1)}, u32[]{:S(2)}, u32[]{:S(2)}) collective-permute-start(bf16[2,128,256]{2,1,0:T(8,128)(2,1)S(1)} %pad_maximum_fusion), channel_id=1, source_target_pairs={{0,4},{1,5},{2,6},{3,7},{4,0},{5,1},{6,2},{7,3},{8,12},{9,13},{10,... | collective-permute-start | bytes 393224 | tf_op jit(solution)/shard_map/ppermute | solution.py:89
  38.6 53.7 %all-to-all-start = ((bf16[256,2,32,128]{3,2,1,0:T(8,128)(2,1)}), bf16[256,2,32,128]{3,2,1,0:T(8,128)(2,1)}, u32[]{:S(2)}, u32[]{:S(2)}) async-start(bf16[256,2,32,128]{3,2,1,0:T(8,128)(2,1)} %bitcast.125), calls=%async_computation | async-start | bytes 8388608 | tf_op jit(solution)/shard_map/all_to_all | solution.py:104
  43.1 7.2 %copy-start.12 = (s32[4]{0:T(128)S(1)}, s32[4]{0:T(128)}, u32[]{:S(2)}) copy-start(s32[4]{0:T(128)} %constant.58.clone) | copy-start | bytes 52
  43.1 8.4 %copy-start.11 = (s32[4]{0:T(128)S(1)}, s32[4]{0:T(128)}, u32[]{:S(2)}) copy-start(s32[4]{0:T(128)} %constant.59.clone) | copy-start | bytes 52
  43.1 9.7 %copy-start.10 = (s32[4]{0:T(128)S(1)}, s32[4]{0:T(128)}, u32[]{:S(2)}) copy-start(s32[4]{0:T(128)} %constant.60.clone) | copy-start | bytes 52
  43.2 10.9 %copy-start.9 = (s32[4]{0:T(128)S(1)}, s32[4]{0:T(128)}, u32[]{:S(2)}) copy-start(s32[4]{0:T(128)} %constant.61.clone) | copy-start | bytes 52
  45.5 72.3 %collective-permute-start.5 = (bf16[96,8192]{1,0:T(8,128)(2,1)}, bf16[96,8192]{1,0:T(8,128)(2,1)}, u32[]{:S(2)}, u32[]{:S(2)}) collective-permute-start(bf16[96,8192]{1,0:T(8,128)(2,1)} %bitcast.64), channel_id=1, source_target_pairs={{0,8},{8,16},{16,24},{24,0},{1,9},{9,17},{17,25},{25,1},{2,10},{10... | collective-permute-start | bytes 4718600 | tf_op jit(solution)/shard_map/ppermute | solution.py:81
  45.5 72.3 %collective-permute-start.6 = (bf16[96,8192]{1,0:T(8,128)(2,1)}, bf16[96,8192]{1,0:T(8,128)(2,1)}, u32[]{:S(2)}, u32[]{:S(2)}) collective-permute-start(bf16[96,8192]{1,0:T(8,128)(2,1)} %bitcast.64), channel_id=1, source_target_pairs={{0,16},{24,8},{1,17},{25,9},{2,18},{26,10},{3,19},{27,11},{4,20},{... | collective-permute-start | bytes 4718600 | tf_op jit(solution)/shard_map/ppermute | solution.py:81
  99.1 4.3 %copy-start.1 = (bf16[16,8,32,256]{3,1,2,0:T(8,128)(2,1)S(1)}, bf16[16,8,32,256]{3,1,2,0:T(8,128)(2,1)}, u32[]{:S(2)}) copy-start(bf16[16,8,32,256]{3,1,2,0:T(8,128)(2,1)} %copy.46) | copy-start | bytes 6291460
  106.2 1.0 copy-start.3
  114.4 4.9 %copy-start = (bf16[32,8,32,256]{3,1,2,0:T(8,128)(2,1)}, bf16[32,8,32,256]{3,1,2,0:T(8,128)(2,1)S(1)}, u32[]{:S(2)}) copy-start(bf16[32,8,32,256]{3,1,2,0:T(8,128)(2,1)S(1)} %copy.44) | copy-start | bytes 12582916
  120.9 1.7 %copy-start.2 = (bf16[192,8192]{1,0:T(8,128)(2,1)}, bf16[192,8192]{1,0:T(8,128)(2,1)S(1)}, u32[]{:S(2)}) copy-start(bf16[192,8192]{1,0:T(8,128)(2,1)S(1)} %constant_dynamic-update-slice_fusion.8) | copy-start | bytes 9437188
  120.9 1.8 %slice-start.1 = ((f32[192,128]{1,0:T(8,128)}), f32[64,128]{1,0:T(8,128)S(1)}, s32[]{:S(2)}) async-start(f32[192,128]{1,0:T(8,128)} %copy-done.3), calls=%async_computation.3 | async-start | bytes 65536 | tf_op jit(solution)/shard_map/slice | solution.py:115
  122.8 7.8 %collective-permute-start.8 = (f32[128,128]{0,1:T(8,128)S(1)}, f32[128,128]{0,1:T(8,128)S(1)}, u32[]{:S(2)}, u32[]{:S(2)}) collective-permute-start(f32[128,128]{0,1:T(8,128)S(1)} %pad_maximum_fusion.3), channel_id=1, source_target_pairs={{16,0},{8,24},{17,1},{9,25},{18,2},{10,26},{19,3},{11,27},{20,4},{... | collective-permute-start | bytes 196616 | tf_op jit(solution)/shard_map/ppermute | solution.py:144
  124.3 6.0 %slice-start = ((f32[192,128]{1,0:T(8,128)}), f32[128,128]{1,0:T(8,128)S(1)}, s32[]{:S(2)}) async-start(f32[192,128]{1,0:T(8,128)} %copy-done.3), calls=%async_computation.2 | async-start | bytes 131072 | tf_op jit(solution)/shard_map/slice | solution.py:114
  124.3 6.2 %collective-permute-start.7 = (f32[128,128]{0,1:T(8,128)S(1)}, f32[128,128]{0,1:T(8,128)S(1)}, u32[]{:S(2)}, u32[]{:S(2)}) collective-permute-start(f32[128,128]{0,1:T(8,128)S(1)} %pad_maximum_fusion.2), channel_id=1, source_target_pairs={{8,0},{16,8},{24,16},{0,24},{9,1},{17,9},{25,17},{1,25},{10,2},{18... | collective-permute-start | bytes 196616 | tf_op jit(solution)/shard_map/ppermute | solution.py:144
